TPU v7x, 512 devices: a whole 4x4x16 slice. The times are simulated.
512 devices in a mesh: dp: 16 (over z), expert: 32 (over x, y, core).
Axes of the slice: x: 4, y: 4, z: 16, core: 2. Of those that a mesh axis runs over, the one named last changes fastest.
Arguments:
- x_tokens: bfloat16 [65536, 2048], P(('dp', 'expert')), may hold values from -6 to 6
- grad_out: bfloat16 [65536, 2048], P(('dp', 'expert')), may hold values from -6 to 6
- expert_ids: int32 [65536, 2], P(('dp', 'expert')), may hold values from 0 to 31, all different within a row; in each aligned block of 128 rows (0 to 127, 128 to 255, ...) at most 10 rows name the same one
- route_probs: float32 [65536, 2], P(('dp', 'expert')), may hold values from 0.1 to 1
- w_gate: bfloat16 [32, 2048, 768], P('expert', 'dp'), may hold values from -0.125 to 0.125
- w_up: bfloat16 [32, 2048, 768], P('expert', 'dp'), may hold values from -0.125 to 0.125
- w_down: bfloat16 [32, 2048, 768], P('expert', 'dp'), may hold values from -0.21875 to 0.21875
Outputs:
- grad_x: bfloat16 [65536, 2048], P(('dp', 'expert'))
- grad_probs: bfloat16 [65536, 2], P(('dp', 'expert'))
- grad_w_down: bfloat16 [32, 2048, 768], P('expert', 'dp')
Inputs may be any that keep to these rules, and one draw needn't show every extreme that they name: `expert_ids`: each token names 2 different experts; among the 128 tokens of one device no expert is named by more than 10 routes, and in every draw some device names some expert exactly 10 times.
All inputs are finite; a program needn't handle non-finite values.
Results may differ from a plain program's by a relative error of at most 0.017.
Values may be sent and summed in bfloat16 or wider, within the bound.
No kernel may reach another device: no remote copies, remote signals or barrier semaphores. Data moves between devices by JAX's collectives and lax.ppermute only.
A program may use at most 64 MiB of HBM per device.

v0:
```python
import jax
import jax.numpy as jnp
from jax import lax
from jax.sharding import PartitionSpec as P


def per_device(x_tokens, grad_out, expert_ids, route_probs, w_gate, w_up, w_down):
    tok_count, model_width = x_tokens.shape
    top_count = expert_ids.shape[1]
    n_expert = lax.axis_size("expert")
    capacity = tok_count * top_count * 5 // (4 * n_expert)
    slot_count = n_expert * capacity
    routes = tok_count * top_count
    flat_ids = expert_ids.reshape(routes)
    onehot = (flat_ids[:, None] == jnp.arange(n_expert, dtype=jnp.int32)).astype(jnp.int32)
    route_rank = jnp.sum((jnp.cumsum(onehot, axis=0) - onehot) * onehot, axis=1)
    target = flat_ids * capacity + route_rank
    source = (
        jnp.full((slot_count,), routes, jnp.int32)
        .at[target]
        .set(jnp.arange(routes, dtype=jnp.int32))
    )
    token_of = jnp.where(source < routes, source // top_count, tok_count)
    x_padded = jnp.concatenate([x_tokens, jnp.zeros((1, model_width), jnp.bfloat16)], axis=0)
    dy_padded = jnp.concatenate([grad_out, jnp.zeros((1, model_width), jnp.bfloat16)], axis=0)
    p_padded = jnp.concatenate([route_probs.reshape(routes), jnp.zeros((1,), jnp.float32)]).astype(
        jnp.bfloat16
    )
    x_slots = x_padded[token_of].reshape(n_expert, capacity, model_width)
    dy_slots = dy_padded[token_of].reshape(n_expert, capacity, model_width)
    p_slots = p_padded[source].reshape(n_expert, capacity)
    arrived = (
        lax.all_to_all(x_slots, "expert", split_axis=0, concat_axis=0, tiled=True),
        lax.all_to_all(dy_slots, "expert", split_axis=0, concat_axis=0, tiled=True),
        lax.all_to_all(p_slots, "expert", split_axis=0, concat_axis=0, tiled=True),
    )
    in_rows = arrived[0].reshape(slot_count, model_width)
    dy_rows = arrived[1].reshape(slot_count, model_width)
    p_rows = arrived[2].reshape(slot_count).astype(jnp.float32)
    scaled = (p_rows[:, None] * dy_rows.astype(jnp.float32)).astype(jnp.bfloat16)
    gate_full, up_full = (
        lax.all_gather(w_gate, "dp", axis=1, tiled=True),
        lax.all_gather(w_up, "dp", axis=1, tiled=True),
    )
    gate_full = gate_full[0]
    up_full = up_full[0]
    gate_pre = jnp.dot(in_rows, gate_full, preferred_element_type=jnp.float32)
    up_pre = jnp.dot(in_rows, up_full, preferred_element_type=jnp.float32)
    gate_sig = jax.nn.sigmoid(gate_pre)
    gate_act = gate_pre * gate_sig
    hidden = (gate_act * up_pre).astype(jnp.bfloat16)
    piece_rows = lax.all_gather(w_down, "dp", axis=1, tiled=True)[0]
    out_piece = jnp.dot(hidden, piece_rows.T, preferred_element_type=jnp.float32)
    grad_sum = jnp.dot(scaled, piece_rows, preferred_element_type=jnp.float32)
    prob_sum = jnp.sum(dy_rows.astype(jnp.float32) * out_piece, axis=1)
    hidden_grad, prob_sum = (grad_sum, prob_sum)
    up_grad = (hidden_grad * gate_act).astype(jnp.bfloat16)
    gate_grad = (hidden_grad * up_pre * gate_sig * (1.0 + gate_pre * (1.0 - gate_sig))).astype(
        jnp.bfloat16
    )
    x_grad = (
        jnp.dot(gate_grad, gate_full.T, preferred_element_type=jnp.float32)
        + jnp.dot(up_grad, up_full.T, preferred_element_type=jnp.float32)
    ).astype(jnp.bfloat16)
    down_grad = lax.psum_scatter(
        lax.dot_general(
            scaled, hidden, (((0,), (0,)), ((), ())), preferred_element_type=jnp.float32
        ).astype(jnp.bfloat16),
        "dp",
        scatter_dimension=0,
        tiled=True,
    )
    grad_w_down = down_grad[None]
    returned = (
        lax.all_to_all(
            x_grad.reshape(n_expert, capacity, model_width),
            "expert",
            split_axis=0,
            concat_axis=0,
            tiled=True,
        ),
        lax.all_to_all(
            prob_sum.astype(jnp.bfloat16).reshape(n_expert, capacity),
            "expert",
            split_axis=0,
            concat_axis=0,
            tiled=True,
        ),
    )
    grad_slots = returned[0].reshape(slot_count, model_width)
    prob_slots = returned[1].reshape(slot_count)
    picked = grad_slots[target].astype(jnp.float32).reshape(tok_count, top_count, model_width)
    grad_x = jnp.sum(picked, axis=1).astype(jnp.bfloat16)
    grad_probs = prob_slots[target].reshape(tok_count, top_count)
    return (grad_x, grad_probs, grad_w_down)


def solution(mesh):
    return jax.shard_map(
        per_device,
        mesh=mesh,
        in_specs=(
            P(("dp", "expert"), None),
            P(("dp", "expert"), None),
            P(("dp", "expert"), None),
            P(("dp", "expert"), None),
            P("expert", "dp", None),
            P("expert", "dp", None),
            P("expert", "dp", None),
        ),
        out_specs=(P(("dp", "expert"), None), P(("dp", "expert"), None), P("expert", "dp", None)),
        check_vma=False,
    )
```

profile of v0, /device:TPU:4, one launch (start us, length us, event | category | flops | bytes accessed | tf_op | source)
XLA Modules:
  0.0 322.4 jit_solution(13100136976467206266)
XLA Ops:
  7.2 0.0 all-gather.8.cloned.1.call-start
  7.2 0.7 all-gather.8.cloned.1.call-update
  7.9 0.0 all-gather.6.cloned.1.call-start
  8.0 0.7 all-gather.6.cloned.1.call-update
  8.7 0.0 all-gather.4.cloned.1.call-start
  8.7 0.7 all-gather.4.cloned.1.call-update
  9.4 0.8 copy.18
  10.2 0.1 eq.29
  10.3 0.1 eq.25
  10.5 0.7 convert.9
  11.1 0.1 copy.16
  11.3 0.1 reshape.120
  11.4 0.7 broadcast_multiply_fusion
  12.1 0.1 copy.17
  12.2 0.1 mul.58
  12.4 0.6 reduce-window.6
  13.0 0.2 slice_reduce_fusion
  13.2 0.1 fusion.30
  13.3 1.4 scatter_custom_fusion
  14.8 2.5 gather_fusion
  17.3 0.7 all_to_all.25
  18.0 9.4 %all-to-all-start = ((bf16[32,1,10]{2,1,0:T(2,128)(2,1)}), bf16[32,1,10]{2,1,0:T(2,128)(2,1)S(1)}, u32[]{:S(2)}, u32[]{:S(2)}) async-start(bf16[32,1,10]{2,1,0:T(2,128)(2,1)} %all_to_all.25), calls=%async_computation | async-start | bytes 32768 | tf_op jit(solution)/shard_map/all_to_all | solution.py:35
  27.5 2.4 gather_fusion.2
  29.9 1.7 reshape.123
  31.6 1.1 all-to-all-done
  32.7 6.4 %all-to-all-start.2 = ((bf16[32,10,2048]{2,1,0:T(8,128)(2,1)}), bf16[32,10,2048]{2,1,0:T(8,128)(2,1)S(1)}, u32[]{:S(2)}, u32[]{:S(2)}) async-start(bf16[32,10,2048]{2,1,0:T(8,128)(2,1)} %reshape.123), calls=%async_computation.2 | async-start | bytes 4194304 | tf_op jit(solution)/shard_map/all_to_all | solution.py:33
  39.2 3.0 gather_fusion.1
  42.2 3.3 %reshape.122 = bf16[32,10,2048]{2,1,0:T(8,128)(2,1)} reshape(bf16[320,2048]{1,0:T(8,128)(2,1)} %gather_fusion.1) | data formatting | bytes 2621440 | tf_op jit(solution)/shard_map/reshape | solution.py:30
  45.6 19.5 %all-to-all-done.2 = bf16[32,10,2048]{2,1,0:T(8,128)(2,1)S(1)} async-done(((bf16[32,10,2048]{2,1,0:T(8,128)(2,1)}), bf16[32,10,2048]{2,1,0:T(8,128)(2,1)S(1)}, u32[]{:S(2)}, u32[]{:S(2)}) %all-to-all-start.2) | async-done | bytes 1310752 | tf_op jit(solution)/shard_map/all_to_all | solution.py:33
  65.0 7.7 %all-to-all-start.1 = ((bf16[32,10,2048]{2,1,0:T(8,128)(2,1)}), bf16[32,10,2048]{2,1,0:T(8,128)(2,1)}, u32[]{:S(2)}, u32[]{:S(2)}) async-start(bf16[32,10,2048]{2,1,0:T(8,128)(2,1)} %reshape.122), calls=%async_computation.1 | async-start | bytes 4194304 | tf_op jit(solution)/shard_map/all_to_all | solution.py:34
  72.7 0.2 reduce-scatter.2.cloned.1.call-start
  73.0 0.1 convert_reduce_fusion
  73.0 0.1 reshape.131
  73.1 1.4 reshape.124
  74.5 24.1 %all-to-all-done.1 = bf16[32,10,2048]{2,1,0:T(8,128)(2,1)} async-done(((bf16[32,10,2048]{2,1,0:T(8,128)(2,1)}), bf16[32,10,2048]{2,1,0:T(8,128)(2,1)}, u32[]{:S(2)}, u32[]{:S(2)}) %all-to-all-start.1) | async-done | bytes 1310752 | tf_op jit(solution)/shard_map/all_to_all | solution.py:34
  98.6 2.5 reshape.130
  101.1 4.4 %fusion.2 = f32[320,768]{1,0:T(8,128)} fusion(bf16[320,2048]{1,0:T(8,128)(2,1)} %reshape.124, bf16[1,2048,768]{2,1,0:T(8,128)(2,1)} %all-gather.8.cloned.1.call-done), kind=kOutput, calls=%fused_computation.10 | convolution fusion | flops 1006632960 | bytes 5439488 | tf_op jit(solution)/shard_map/dot_general | solution.py:47
  105.6 58.7 %all-gather.6.cloned.1.call-done = bf16[1,2048,768]{2,1,0:T(8,128)(2,1)} async-done(((bf16[1,128,768]{2,1,0:T(8,128)(2,1)}), bf16[1,2048,768]{2,1,0:T(8,128)(2,1)}) %all-gather.6.cloned.1.call-update) | async-done | bytes 3145744 | tf_op jit(solution)/shard_map/all_gather | solution.py:43
  164.3 4.7 %multiply_convert_fusion.3 = (bf16[320,768]{1,0:T(8,128)(2,1)S(1)}, f32[320,768]{1,0:T(8,128)}) fusion(f32[320,768]{1,0:T(8,128)} %fusion.2, bf16[320,2048]{1,0:T(8,128)(2,1)} %reshape.124, bf16[1,2048,768]{2,1,0:T(8,128)(2,1)} %all-gather.6.cloned.1.call-done), kind=kOutput, calls=%fused_computation.26 | convolution fusion | flops 1008107520 | bytes 6914048 | tf_op jit(solution)/shard_map/dot_general | solution.py:48
  169.0 3.6 %convolution_convert_fusion = bf16[2048,768]{1,0:T(8,128)(2,1)} fusion(bf16[320,768]{1,0:T(8,128)(2,1)S(1)} %get-tuple-element.11, f32[320,2048]{1,0:T(8,128)S(1)} %reshape.130, f32[320]{0:T(512)S(1)} %reshape.131), kind=kOutput, calls=%fused_computation.7 | convolution fusion | flops 1009516544 | bytes 6259968 | tf_op jit(solution)/shard_map/dot_general | solution.py:66
  172.6 3.3 %multiply_convert_fusion = bf16[32,10,2048]{2,1,0:T(8,128)(2,1)} fusion(f32[32,10]{1,0:T(8,128)S(1)} %bitcast.54, bf16[32,10,2048]{2,1,0:T(8,128)(2,1)} %all-to-all-done.1), kind=kLoop, calls=%fused_computation.6 | loop fusion | flops 1966080 | bytes 2622720 | tf_op jit(solution)/shard_map/convert_element_type | solution.py:40
  175.9 3.6 %convert_element_type.80 = bf16[320,2048]{1,0:T(8,128)(2,1)} reshape(bf16[32,10,2048]{2,1,0:T(8,128)(2,1)} %multiply_convert_fusion) | data formatting | bytes 2621440 | tf_op jit(solution)/shard_map/convert_element_type | solution.py:40
  179.5 59.1 %all-gather.4.cloned.1.call-done = bf16[1,2048,768]{2,1,0:T(8,128)(2,1)} async-done(((bf16[1,128,768]{2,1,0:T(8,128)(2,1)}), bf16[1,2048,768]{2,1,0:T(8,128)(2,1)}) %all-gather.4.cloned.1.call-update) | async-done | bytes 3145744 | tf_op jit(solution)/shard_map/all_gather | solution.py:52
  238.7 3.2 fusion.21
  241.9 0.7 convert_element_type.96
  242.6 7.4 %all-to-all-start.4 = ((bf16[32,1,10]{2,1,0:T(2,128)(2,1)}), bf16[32,1,10]{2,1,0:T(2,128)(2,1)S(1)}, u32[]{:S(2)}, u32[]{:S(2)}) async-start(bf16[32,1,10]{2,1,0:T(2,128)(2,1)} %convert_element_type.96), calls=%async_computation.4 | async-start | bytes 32768 | tf_op jit(solution)/shard_map/all_to_all | solution.py:82
  250.1 3.6 %fusion.10 = f32[320,768]{1,0:T(8,128)S(1)} fusion(bf16[320,2048]{1,0:T(8,128)(2,1)} %convert_element_type.80, bf16[1,2048,768]{2,1,0:T(8,128)(2,1)} %all-gather.4.cloned.1.call-done), kind=kOutput, calls=%fused_computation.18 | convolution fusion | flops 1006632960 | bytes 5439488 | tf_op jit(solution)/shard_map/dot_general | solution.py:54
  253.7 0.1 copy-done.5
  253.8 1.3 fusion
  255.2 0.7 copy-done.3
  255.8 1.2 fusion.18
  257.0 1.6 reshape.125
  258.6 7.4 %all-to-all-start.3 = ((bf16[32,10,2048]{2,1,0:T(8,128)(2,1)}), bf16[32,10,2048]{2,1,0:T(8,128)(2,1)S(1)}, u32[]{:S(2)}, u32[]{:S(2)}) async-start(bf16[32,10,2048]{2,1,0:T(8,128)(2,1)} %reshape.125), calls=%async_computation.3 | async-start | bytes 4194304 | tf_op jit(solution)/shard_map/all_to_all | solution.py:75
  266.0 0.1 reduce.2
  266.1 0.1 reshape.127
  266.2 1.9 gather_fusion.4
  268.1 0.2 reshape.128
  268.3 0.6 copy.23
  268.9 23.0 %all-to-all-done.3 = bf16[32,10,2048]{2,1,0:T(8,128)(2,1)S(1)} async-done(((bf16[32,10,2048]{2,1,0:T(8,128)(2,1)}), bf16[32,10,2048]{2,1,0:T(8,128)(2,1)S(1)}, u32[]{:S(2)}, u32[]{:S(2)}) %all-to-all-start.3) | async-done | bytes 1310752 | tf_op jit(solution)/shard_map/all_to_all | solution.py:75
  291.9 0.5 reshape.126
  292.4 1.4 gather_fusion.3
  293.8 0.7 gather.21
  294.5 3.6 %reduce_sum.34 = bf16[128,2048]{1,0:T(8,128)(2,1)} reduce(bf16[128,2,2048]{2,1,0:T(2,128)(2,1)S(1)} %gather.21, bf16[]{:T(256)} %constant.36.clone.1), dimensions={1}, to_apply=%region_4.5 | reduce | flops 262144 | bytes 1572866 | tf_op jit(solution)/shard_map/reduce_sum | solution.py:93
  298.1 17.8 %reduce-scatter.2.cloned.1.call-done = bf16[128,768]{1,0:T(8,128)(2,1)} async-done(((bf16[2048,768]{1,0:T(8,128)(2,1)}), bf16[128,768]{1,0:T(8,128)(2,1)}) %reduce-scatter.2.cloned.1.call-update) | async-done | bytes 196624 | tf_op jit(solution)/shard_map/reduce_scatter | solution.py:65
  (25 shorter events, 0.3 us)
Async XLA Ops:
  7.2 20.3 %copy-start = (bf16[128,2048]{1,0:T(8,128)(2,1)S(1)}, bf16[128,2048]{1,0:T(8,128)(2,1)}, u32[]{:S(2)}) copy-start(bf16[128,2048]{1,0:T(8,128)(2,1)} %param.7) | copy-start | bytes 1572868
  7.2 94.0 %all-gather.8.cloned.1.call-start = ((), (), s32[]{:S(2)}) async-start(), calls=%async_computation.8 | async-start | bytes 3342336 | tf_op jit(solution)/shard_map/all_gather | solution.py:42
  7.9 156.4 %all-gather.6.cloned.1.call-start = ((), (), s32[]{:S(2)}) async-start(), calls=%async_computation.7 | async-start | bytes 3342336 | tf_op jit(solution)/shard_map/all_gather | solution.py:43
  8.7 230.0 %all-gather.4.cloned.1.call-start = ((), (), s32[]{:S(2)}) async-start(), calls=%async_computation.6 | async-start | bytes 3342336 | tf_op jit(solution)/shard_map/all_gather | solution.py:52
  18.0 14.7 %all-to-all-start = ((bf16[32,1,10]{2,1,0:T(2,128)(2,1)}), bf16[32,1,10]{2,1,0:T(2,128)(2,1)S(1)}, u32[]{:S(2)}, u32[]{:S(2)}) async-start(bf16[32,1,10]{2,1,0:T(2,128)(2,1)} %all_to_all.25), calls=%async_computation | async-start | bytes 32768 | tf_op jit(solution)/shard_map/all_to_all | solution.py:35
  31.6 7.5 %copy-start.1 = (bf16[128,2048]{1,0:T(8,128)(2,1)S(1)}, bf16[128,2048]{1,0:T(8,128)(2,1)}, u32[]{:S(2)}) copy-start(bf16[128,2048]{1,0:T(8,128)(2,1)} %param.8) | copy-start | bytes 1572868
  32.7 32.4 %all-to-all-start.2 = ((bf16[32,10,2048]{2,1,0:T(8,128)(2,1)}), bf16[32,10,2048]{2,1,0:T(8,128)(2,1)S(1)}, u32[]{:S(2)}, u32[]{:S(2)}) async-start(bf16[32,10,2048]{2,1,0:T(8,128)(2,1)} %reshape.123), calls=%async_computation.2 | async-start | bytes 4194304 | tf_op jit(solution)/shard_map/all_to_all | solution.py:33
  65.0 33.6 %all-to-all-start.1 = ((bf16[32,10,2048]{2,1,0:T(8,128)(2,1)}), bf16[32,10,2048]{2,1,0:T(8,128)(2,1)}, u32[]{:S(2)}, u32[]{:S(2)}) async-start(bf16[32,10,2048]{2,1,0:T(8,128)(2,1)} %reshape.122), calls=%async_computation.1 | async-start | bytes 4194304 | tf_op jit(solution)/shard_map/all_to_all | solution.py:34
  72.7 243.2 %reduce-scatter.2.cloned.1.call-start = ((), (), s32[]{:S(2)}) async-start(), calls=%async_computation.9 | async-start | bytes 3342336 | tf_op jit(solution)/shard_map/reduce_scatter | solution.py:65
  242.6 16.0 %all-to-all-start.4 = ((bf16[32,1,10]{2,1,0:T(2,128)(2,1)}), bf16[32,1,10]{2,1,0:T(2,128)(2,1)S(1)}, u32[]{:S(2)}, u32[]{:S(2)}) async-start(bf16[32,1,10]{2,1,0:T(2,128)(2,1)} %convert_element_type.96), calls=%async_computation.4 | async-start | bytes 32768 | tf_op jit(solution)/shard_map/all_to_all | solution.py:82
  250.0 3.6 %copy-start.2 = (bf16[1,2048,768]{2,1,0:T(8,128)(2,1)S(1)}, bf16[1,2048,768]{2,1,0:T(8,128)(2,1)}, u32[]{:S(2)}) copy-start(bf16[1,2048,768]{2,1,0:T(8,128)(2,1)} %all-gather.8.cloned.1.call-done) | copy-start | bytes 9437188
  250.0 3.6 %copy-start.4 = (f32[320,768]{1,0:T(8,128)S(1)}, f32[320,768]{1,0:T(8,128)}, u32[]{:S(2)}) copy-start(f32[320,768]{1,0:T(8,128)} %fusion.2) | copy-start | bytes 2949124
  250.0 3.8 %copy-start.5 = (f32[320,768]{1,0:T(8,128)S(1)}, f32[320,768]{1,0:T(8,128)}, u32[]{:S(2)}) copy-start(f32[320,768]{1,0:T(8,128)} %get-tuple-element.12) | copy-start | bytes 2949124
  253.8 2.0 copy-start.3
  258.6 33.3 %all-to-all-start.3 = ((bf16[32,10,2048]{2,1,0:T(8,128)(2,1)}), bf16[32,10,2048]{2,1,0:T(8,128)(2,1)S(1)}, u32[]{:S(2)}, u32[]{:S(2)}) async-start(bf16[32,10,2048]{2,1,0:T(8,128)(2,1)} %reshape.125), calls=%async_computation.3 | async-start | bytes 4194304 | tf_op jit(solution)/shard_map/all_to_all | solution.py:75
Sparse Core Ops, SparseCore 0:
  10.1 79.8 all-gather.7
  92.0 72.2 all-gather.5
  166.4 72.2 all-gather.3
  241.9 73.9 reduce-scatter.1
where the time goes:
time: 323 us; the launch traced here: 322 us
  waiting for transfers between devices  205 us (63%)
  starting transfers between devices  38.7 us (12%)
  local copies, waits for them, and re-layouts  32.9 us (10%)
  matrix products  22.1 us (7%)
  between operations  14.1 us (4%)
  other arithmetic  9.22 us (3%)
    all_gather x1, waiting for transfers between devices, per_device(): piece_rows = lax.all_gather(w_down, 'dp', axis=1, tiled=True)[0]  59.1 us
    all_gather x1, waiting for transfers between devices, per_device(): lax.all_gather(w_up, 'dp', axis=1, tiled=True)  58.7 us
    all_to_all x1, waiting for transfers between devices, per_device(): lax.all_to_all(dy_slots, 'expert', split_axis=0, concat_axis=0, tiled=True)  24.1 us
    all_to_all x1, waiting for transfers between devices, per_device(): lax.all_to_all(x_grad.reshape(n_expert, capacity, model_width), 'expert',...  23 us
    all_to_all x1, waiting for transfers between devices, per_device(): lax.all_to_all(x_slots, 'expert', split_axis=0, concat_axis=0, tiled=True)  19.5 us
    reduce_scatter x1, waiting for transfers between devices, per_device(): lax.psum_scatter(lax.dot_general(scaled, hidden, (((0,), (0,)), ((), ()))...  17.8 us
    all_to_all x1, starting transfers between devices, per_device(): lax.all_to_all(p_slots, 'expert', split_axis=0, concat_axis=0, tiled=True)  9.43 us
    all_to_all x1, starting transfers between devices, per_device(): lax.all_to_all(dy_slots, 'expert', split_axis=0, concat_axis=0, tiled=True)  7.69 us
  transfers between devices with their start and end apart: 9, of which 7 were waited for; matrix products, arithmetic and copies ran while one was open for 19% of the time, Pallas kernels for 0%

commit v1 on v0

--- a/solution.py
+++ b/solution.py
@@ -49,7 +49,9 @@
     gate_sig = jax.nn.sigmoid(gate_pre)
     gate_act = gate_pre * gate_sig
     hidden = (gate_act * up_pre).astype(jnp.bfloat16)
-    piece_rows = lax.all_gather(w_down, "dp", axis=1, tiled=True)[0]
+    piece_rows = jnp.concatenate(
+        lax.all_to_all(jnp.stack([w_down] * lax.axis_size("dp")), "dp", 0, 0), axis=1
+    )[0]
     out_piece = jnp.dot(hidden, piece_rows.T, preferred_element_type=jnp.float32)
     grad_sum = jnp.dot(scaled, piece_rows, preferred_element_type=jnp.float32)
     prob_sum = jnp.sum(dy_rows.astype(jnp.float32) * out_piece, axis=1)

time: 323 us -> 380 us (1.18)
  the two profiles are of different devices: /device:TPU:4 before, /device:TPU:2 now
where the time goes in v1:
time: 380 us; the launch traced here: 379 us
  waiting for transfers between devices  223 us (59%)
  starting transfers between devices  42 us (11%)
  local copies, waits for them, and re-layouts  35.8 us (9%)
  blocking collectives  33.4 us (9%)
  matrix products  22.1 us (6%)
  between operations  14 us (4%)
  other arithmetic  9.21 us (2%)
    all_gather x1, waiting for transfers between devices, per_device(): lax.all_gather(w_up, 'dp', axis=1, tiled=True)  169 us
    all_to_all x1, blocking collectives, per_device(): lax.all_to_all(dy_slots, 'expert', split_axis=0, concat_axis=0, tiled=True)  33.4 us
    all_to_all x1, waiting for transfers between devices, per_device(): lax.all_to_all(x_grad.reshape(n_expert, capacity, model_width), 'expert',...  23 us
    all_to_all x1, waiting for transfers between devices, per_device(): lax.all_to_all(x_slots, 'expert', split_axis=0, concat_axis=0, tiled=True)  19.5 us
    all_to_all x1, starting transfers between devices, per_device(): lax.all_to_all(jnp.stack([w_down] * lax.axis_size('dp')), 'dp', 0, 0)  13.4 us
    all_to_all x1, starting transfers between devices, per_device(): lax.all_to_all(p_slots, 'expert', split_axis=0, concat_axis=0, tiled=True)  9.41 us
    reduce_scatter x1, waiting for transfers between devices, per_device(): lax.psum_scatter(lax.dot_general(scaled, hidden, (((0,), (0,)), ((), ()))...  8.8 us
  transfers between devices with their start and end apart: 8, of which 5 were waited for; matrix products, arithmetic and copies ran while one was open for 17% of the time, Pallas kernels for 0%

profile of v1, /device:TPU:2, one launch (start us, length us, event | category | flops | bytes accessed | tf_op | source)
XLA Modules:
  0.0 379.4 jit_solution(1607836383480812416)
XLA Ops:
  7.2 0.0 all-gather.5.cloned.1.call-start
  7.2 0.7 all-gather.5.cloned.1.call-update
  7.9 0.8 copy.18
  8.7 0.1 eq.25
  8.8 0.1 eq.29
  9.0 0.7 broadcast_multiply_fusion
  9.7 0.1 copy.17
  9.8 0.1 mul.58
  9.9 0.6 reduce-window.6
  10.5 0.2 slice_reduce_fusion
  10.7 0.7 convert.9
  11.4 0.1 copy.16
  11.6 0.1 reshape.123
  11.7 0.1 fusion.21
  11.8 1.4 scatter_custom_fusion
  13.3 2.5 gather_fusion
  15.8 0.7 all_to_all.29
  16.5 9.4 %all-to-all-start = ((bf16[32,1,10]{2,1,0:T(2,128)(2,1)}), bf16[32,1,10]{2,1,0:T(2,128)(2,1)S(1)}, u32[]{:S(2)}, u32[]{:S(2)}) async-start(bf16[32,1,10]{2,1,0:T(2,128)(2,1)} %all_to_all.29), calls=%async_computation | async-start | bytes 32768 | tf_op jit(solution)/shard_map/all_to_all | solution.py:35
  25.9 1.1 concatenate.12
  27.0 2.4 gather_fusion.2
  29.4 1.6 reshape.126
  31.0 1.1 all-to-all-done
  32.1 6.5 %all-to-all-start.3 = ((bf16[32,10,2048]{2,1,0:T(8,128)(2,1)}), bf16[32,10,2048]{2,1,0:T(8,128)(2,1)S(1)}, u32[]{:S(2)}, u32[]{:S(2)}) async-start(bf16[32,10,2048]{2,1,0:T(8,128)(2,1)} %reshape.126), calls=%async_computation.3 | async-start | bytes 4194304 | tf_op jit(solution)/shard_map/all_to_all | solution.py:33
  38.7 3.0 gather_fusion.1
  41.7 3.4 reshape.125
  45.1 19.5 %all-to-all-done.3 = bf16[32,10,2048]{2,1,0:T(8,128)(2,1)S(1)} async-done(((bf16[32,10,2048]{2,1,0:T(8,128)(2,1)}), bf16[32,10,2048]{2,1,0:T(8,128)(2,1)S(1)}, u32[]{:S(2)}, u32[]{:S(2)}) %all-to-all-start.3) | async-done | bytes 1310752 | tf_op jit(solution)/shard_map/all_to_all | solution.py:33
  64.5 33.4 %all_to_all.36 = bf16[32,10,2048]{2,1,0:T(8,128)(2,1)} all-to-all(bf16[32,10,2048]{2,1,0:T(8,128)(2,1)} %reshape.125), channel_id=1, replica_groups=mesh['dp'=16,'expert'=32] {'expert'}, dimensions={0} | all-to-all | bytes 2621440 | tf_op jit(solution)/shard_map/all_to_all | solution.py:34
  98.0 2.0 stack.2
  99.9 13.4 %all-to-all-start.2 = ((bf16[16,1,128,768]{3,2,1,0:T(8,128)(2,1)}), bf16[16,1,128,768]{3,2,1,0:T(8,128)(2,1)}, u32[]{:S(2)}, u32[]{:S(2)}) async-start(bf16[16,1,128,768]{3,2,1,0:T(8,128)(2,1)} %stack.2), calls=%async_computation.2 | async-start | bytes 6291456 | tf_op jit(solution)/shard_map/all_to_all | solution.py:53
  113.3 0.0 all-gather.3.cloned.1.call-start
  113.4 0.7 all-gather.3.cloned.1.call-update
  114.1 0.2 reduce-scatter.2.cloned.1.call-start
  114.3 0.1 convert_reduce_fusion
  114.4 0.1 reshape.134
  114.5 1.3 reshape.127
  115.8 2.5 reshape.133
  118.3 0.0 all-gather.5.cloned.1.call-done
  118.3 4.4 %fusion.2 = f32[320,768]{1,0:T(8,128)} fusion(bf16[320,2048]{1,0:T(8,128)(2,1)} %reshape.127, bf16[1,2048,768]{2,1,0:T(8,128)(2,1)} %all-gather.5.cloned.1.call-done), kind=kOutput, calls=%fused_computation.10 | convolution fusion | flops 1006632960 | bytes 5439488 | tf_op jit(solution)/shard_map/dot_general | solution.py:47
  122.7 169.0 %all-gather.3.cloned.1.call-done = bf16[1,2048,768]{2,1,0:T(8,128)(2,1)} async-done(((bf16[1,128,768]{2,1,0:T(8,128)(2,1)}), bf16[1,2048,768]{2,1,0:T(8,128)(2,1)}) %all-gather.3.cloned.1.call-update) | async-done | bytes 3145744 | tf_op jit(solution)/shard_map/all_gather | solution.py:43
  291.7 4.7 %multiply_convert_fusion.3 = (bf16[320,768]{1,0:T(8,128)(2,1)S(1)}, f32[320,768]{1,0:T(8,128)}) fusion(f32[320,768]{1,0:T(8,128)} %fusion.2, bf16[320,2048]{1,0:T(8,128)(2,1)} %reshape.127, bf16[1,2048,768]{2,1,0:T(8,128)(2,1)} %all-gather.3.cloned.1.call-done), kind=kOutput, calls=%fused_computation.22 | convolution fusion | flops 1008107520 | bytes 6914048 | tf_op jit(solution)/shard_map/dot_general | solution.py:48
  296.4 3.6 convolution_convert_fusion
  300.1 3.3 multiply_convert_fusion
  303.4 3.6 convert_element_type.80
  307.0 3.2 fusion.14
  310.2 0.7 convert_element_type.96
  311.0 5.0 %all-to-all-start.5 = ((bf16[32,1,10]{2,1,0:T(2,128)(2,1)}), bf16[32,1,10]{2,1,0:T(2,128)(2,1)S(1)}, u32[]{:S(2)}, u32[]{:S(2)}) async-start(bf16[32,1,10]{2,1,0:T(2,128)(2,1)} %convert_element_type.96), calls=%async_computation.5 | async-start | bytes 32768 | tf_op jit(solution)/shard_map/all_to_all | solution.py:84
  316.0 3.6 fusion.30
  319.7 0.2 copy-done.5
  319.8 1.3 fusion
  321.2 0.5 copy-done.3
  321.7 1.2 fusion.11
  322.9 1.6 reshape.128
  324.5 7.4 %all-to-all-start.4 = ((bf16[32,10,2048]{2,1,0:T(8,128)(2,1)}), bf16[32,10,2048]{2,1,0:T(8,128)(2,1)S(1)}, u32[]{:S(2)}, u32[]{:S(2)}) async-start(bf16[32,10,2048]{2,1,0:T(8,128)(2,1)} %reshape.128), calls=%async_computation.4 | async-start | bytes 4194304 | tf_op jit(solution)/shard_map/all_to_all | solution.py:77
  332.0 0.1 reduce.2
  332.0 0.1 reshape.130
  332.1 1.9 gather_fusion.4
  334.1 0.2 reshape.131
  334.2 0.6 copy.23
  334.8 23.0 %all-to-all-done.4 = bf16[32,10,2048]{2,1,0:T(8,128)(2,1)S(1)} async-done(((bf16[32,10,2048]{2,1,0:T(8,128)(2,1)}), bf16[32,10,2048]{2,1,0:T(8,128)(2,1)S(1)}, u32[]{:S(2)}, u32[]{:S(2)}) %all-to-all-start.4) | async-done | bytes 1310752 | tf_op jit(solution)/shard_map/all_to_all | solution.py:77
  357.8 0.5 reshape.129
  358.3 1.4 gather_fusion.3
  359.7 0.7 gather.21
  360.4 3.6 reduce_sum.34
  364.0 8.8 %reduce-scatter.2.cloned.1.call-done = bf16[128,768]{1,0:T(8,128)(2,1)} async-done(((bf16[2048,768]{1,0:T(8,128)(2,1)}), bf16[128,768]{1,0:T(8,128)(2,1)}) %reduce-scatter.2.cloned.1.call-update) | async-done | bytes 196624 | tf_op jit(solution)/shard_map/reduce_scatter | solution.py:67
  (24 shorter events, 0.2 us)
Async XLA Ops:
  7.2 111.2 %all-gather.5.cloned.1.call-start = ((), (), s32[]{:S(2)}) async-start(), calls=%async_computation.8 | async-start | bytes 3342336 | tf_op jit(solution)/shard_map/all_gather | solution.py:42
  16.5 15.6 %all-to-all-start = ((bf16[32,1,10]{2,1,0:T(2,128)(2,1)}), bf16[32,1,10]{2,1,0:T(2,128)(2,1)S(1)}, u32[]{:S(2)}, u32[]{:S(2)}) async-start(bf16[32,1,10]{2,1,0:T(2,128)(2,1)} %all_to_all.29), calls=%async_computation | async-start | bytes 32768 | tf_op jit(solution)/shard_map/all_to_all | solution.py:35
  31.0 7.6 %copy-start = (bf16[128,2048]{1,0:T(8,128)(2,1)S(1)}, bf16[128,2048]{1,0:T(8,128)(2,1)}, u32[]{:S(2)}) copy-start(bf16[128,2048]{1,0:T(8,128)(2,1)} %param.8) | copy-start | bytes 1572868
  32.1 32.4 %all-to-all-start.3 = ((bf16[32,10,2048]{2,1,0:T(8,128)(2,1)}), bf16[32,10,2048]{2,1,0:T(8,128)(2,1)S(1)}, u32[]{:S(2)}, u32[]{:S(2)}) async-start(bf16[32,10,2048]{2,1,0:T(8,128)(2,1)} %reshape.126), calls=%async_computation.3 | async-start | bytes 4194304 | tf_op jit(solution)/shard_map/all_to_all | solution.py:33
  45.1 52.9 %copy-start.1 = (bf16[1,128,768]{2,1,0:T(8,128)(2,1)S(1)}, bf16[1,128,768]{2,1,0:T(8,128)(2,1)}, u32[]{:S(2)}) copy-start(bf16[1,128,768]{2,1,0:T(8,128)(2,1)} %param.13) | copy-start | bytes 589828
  99.9 207.1 %all-to-all-start.2 = ((bf16[16,1,128,768]{3,2,1,0:T(8,128)(2,1)}), bf16[16,1,128,768]{3,2,1,0:T(8,128)(2,1)}, u32[]{:S(2)}, u32[]{:S(2)}) async-start(bf16[16,1,128,768]{3,2,1,0:T(8,128)(2,1)} %stack.2), calls=%async_computation.2 | async-start | bytes 6291456 | tf_op jit(solution)/shard_map/all_to_all | solution.py:53
  113.3 178.4 %all-gather.3.cloned.1.call-start = ((), (), s32[]{:S(2)}) async-start(), calls=%async_computation.7 | async-start | bytes 3342336 | tf_op jit(solution)/shard_map/all_gather | solution.py:43
  114.1 258.8 %reduce-scatter.2.cloned.1.call-start = ((), (), s32[]{:S(2)}) async-start(), calls=%async_computation.9 | async-start | bytes 3342336 | tf_op jit(solution)/shard_map/reduce_scatter | solution.py:67
  311.0 13.6 %all-to-all-start.5 = ((bf16[32,1,10]{2,1,0:T(2,128)(2,1)}), bf16[32,1,10]{2,1,0:T(2,128)(2,1)S(1)}, u32[]{:S(2)}, u32[]{:S(2)}) async-start(bf16[32,1,10]{2,1,0:T(2,128)(2,1)} %convert_element_type.96), calls=%async_computation.5 | async-start | bytes 32768 | tf_op jit(solution)/shard_map/all_to_all | solution.py:84
  316.0 3.6 copy-start.2
  316.0 3.6 copy-start.4
  316.0 3.8 %copy-start.5 = (f32[320,768]{1,0:T(8,128)S(1)}, f32[320,768]{1,0:T(8,128)}, u32[]{:S(2)}) copy-start(f32[320,768]{1,0:T(8,128)} %get-tuple-element.12) | copy-start | bytes 2949124
  319.8 1.9 copy-start.3
  324.5 33.3 %all-to-all-start.4 = ((bf16[32,10,2048]{2,1,0:T(8,128)(2,1)}), bf16[32,10,2048]{2,1,0:T(8,128)(2,1)S(1)}, u32[]{:S(2)}, u32[]{:S(2)}) async-start(bf16[32,10,2048]{2,1,0:T(8,128)(2,1)} %reshape.128), calls=%async_computation.4 | async-start | bytes 4194304 | tf_op jit(solution)/shard_map/all_to_all | solution.py:77
Sparse Core Ops, SparseCore 0:
  10.1 79.8 all-gather.4
  116.2 175.4 all-gather.2
  300.2 72.5 reduce-scatter.1
